TPU v7x, 256 devices: a whole 4x4x8 slice. The times are simulated.
256 devices in a mesh: ctx: 64 (over z, x, core), head: 4 (over y).
Axes of the slice: x: 4, y: 4, z: 8, core: 2. Of those that a mesh axis runs over, the one named last changes fastest.
Arguments:
- queries: bfloat16 [8192, 32, 128], P('ctx', 'head'), may hold values from -14 to 14
- keys: bfloat16 [8192, 32, 128], P('ctx', 'head'), may hold values from -14 to 14
- values: bfloat16 [8192, 32, 128], P('ctx', 'head'), may hold values from -6 to 6
- gain: float32 [32, 128], P('head'), may hold values from 0.1 to 1.9
- doc_lengths: int32 [64], replicated, may hold values from 1 to 2048, 8192 in all
- cotangent: bfloat16 [8192, 32, 128], P('ctx', 'head'), may hold values from -6 to 6
Outputs:
- mixed: bfloat16 [8192, 32, 128], P('ctx', 'head')
- query_grad: bfloat16 [8192, 32, 128], P('ctx', 'head')
- key_grad: bfloat16 [8192, 32, 128], P('ctx', 'head')
- value_grad: bfloat16 [8192, 32, 128], P('ctx', 'head')
All inputs are finite; a program needn't handle non-finite values.
Results may differ from a plain program's by a relative error of at most 0.0054.
Values may be sent and summed in bfloat16 or wider, within the bound.
No kernel may reach another device: no remote copies, remote signals or barrier semaphores. Data moves between devices by JAX's collectives and lax.ppermute only.
A program may use at most 128 MiB of HBM per device.

v0:
```python
import jax
import jax.numpy as jnp
from jax import lax
from jax.sharding import PartitionSpec as P

SPAN = 2
MAXDOC = 2048
neg_large = -1e30
norm_eps = 1e-06


def from_behind(x, axis, by):
    devices = lax.axis_size(axis)
    pairs = [(i, i + by) for i in range(devices) if 0 <= i + by < devices]
    return lax.ppermute(x, axis, pairs)


def send_state(x, axis, by):
    return from_behind(x.astype(jnp.bfloat16), axis, by).astype(jnp.float32)


def tile_state(keys_t, values_t, doc_lengths, start):
    tile = keys_t.shape[0]
    docs = doc_index(doc_lengths, start + jnp.arange(tile, dtype=jnp.int32))
    keep = (docs == docs[tile - 1])[:, None, None]
    return narrow("uhd,uhe->hde", jnp.where(keep, keys_t, jnp.zeros_like(keys_t)), values_t)


def fold_states(pieces, flags):
    total = pieces[0]
    for piece, flag in zip(pieces[1:], flags[1:]):
        total = piece + (1.0 - flag) * total
    return total


def front_flags(doc_lengths, spans, tile):
    low = jnp.stack([lo * tile - 1 for lo, hi in spans])
    high = jnp.stack([hi * tile + tile - 1 for lo, hi in spans])
    docs = doc_index(doc_lengths, jnp.concatenate([low, high]).astype(jnp.int32))
    count = len(spans)
    return (docs[:count] != docs[count:]).astype(jnp.float32)


def back_flags(doc_lengths, spans, tile):
    low = jnp.stack([lo * tile for lo, hi in spans])
    high = jnp.stack([hi * tile + tile for lo, hi in spans])
    docs = doc_index(doc_lengths, jnp.concatenate([low, high]).astype(jnp.int32))
    count = len(spans)
    return (docs[:count] != docs[count:]).astype(jnp.float32)


def wide(form, left, right):
    return jnp.einsum(form, left, right, precision=lax.Precision.HIGHEST)


def narrow(form, left, right):
    return jnp.einsum(form, left, right, preferred_element_type=jnp.float32)


def doc_index(doc_lengths, positions):
    starts = jnp.cumsum(doc_lengths) - doc_lengths
    return jnp.sum((starts[None, :] <= positions[:, None]).astype(jnp.int32), axis=1) - 1


def one_doc(doc_lengths, position):
    return doc_index(doc_lengths, jnp.reshape(position, (1,)))[0]


def masked_scores(query_block, key_block, mask, scale):
    raw = narrow("thd,uhd->htu", query_block, key_block) * scale
    return jnp.where(mask[None], raw, neg_large)


def key_terms(dscores, weights, query_block, grad_block, scale):
    key_part = narrow("htu,thd->uhd", dscores, query_block) * scale
    value_part = narrow("htu,thd->uhd", weights, grad_block)
    return (key_part, value_part)


def per_device(queries, keys, values, gain, doc_lengths, cotangent):
    tile, heads, width = queries.shape
    features = heads * lax.axis_size("head") * width
    scale = width ** (-0.5)
    base = lax.axis_index("ctx") * tile
    offsets = jnp.arange(tile, dtype=jnp.int32)
    own_pos = base + offsets
    own_doc = doc_index(doc_lengths, own_pos)
    prev_doc = one_doc(doc_lengths, base - 1)
    next_doc = one_doc(doc_lengths, base + tile)
    pair = jnp.stack([keys, values])
    arrived = [from_behind(pair, "ctx", shift) for shift in range(SPAN, 0, -1)]
    key_tiles = [piece[0] for piece in arrived] + [keys]
    value_tiles = [piece[1] for piece in arrived] + [values]
    masks = []
    for position in range(SPAN + 1):
        key_pos = base - (SPAN - position) * tile + offsets
        key_doc = doc_index(doc_lengths, key_pos)
        masks.append(
            (own_doc[:, None] == key_doc[None, :]) & (key_pos[None, :] <= own_pos[:, None])
        )
    score_list = [
        masked_scores(queries, key_tiles[position], masks[position], scale)
        for position in range(SPAN + 1)
    ]
    top = score_list[0].max(axis=-1)
    for position in range(1, SPAN + 1):
        top = jnp.maximum(top, score_list[position].max(axis=-1))
    total = jnp.zeros((heads, tile), jnp.float32)
    for position in range(SPAN + 1):
        total = total + jnp.sum(jnp.exp(score_list[position] - top[..., None]), axis=-1)
    log_total = top + jnp.log(total)
    prob_list = []
    weight_list = []
    soft_out = jnp.zeros((tile, heads, width), jnp.float32)
    for position in range(SPAN + 1):
        probs = jnp.exp(score_list[position] - log_total[..., None])
        weights = probs.astype(jnp.bfloat16)
        prob_list.append(probs)
        weight_list.append(weights)
        soft_out = soft_out + narrow("htu,uhd->thd", weights, value_tiles[position])
    same_tile = masks[SPAN].astype(jnp.float32)
    carried_prev = (own_doc == prev_doc).astype(jnp.float32)
    carried_next = (own_doc == next_doc).astype(jnp.float32)
    keep_first = (own_doc == own_doc[0])[:, None, None]
    query_wide = queries.astype(jnp.float32)
    attend = (narrow("thd,uhd->htu", queries, keys) * same_tile).astype(jnp.bfloat16)
    grad_wide = cotangent.astype(jnp.float32)
    row_dot = jnp.sum(grad_wide * soft_out, axis=-1).T
    query_soft = jnp.zeros((tile, heads, width), jnp.float32)
    dscore_list = []
    for position in range(SPAN + 1):
        dprobs = narrow("thd,uhd->htu", cotangent, value_tiles[position])
        dscores = (prob_list[position] * (dprobs - row_dot[..., None])).astype(jnp.bfloat16)
        query_soft = query_soft + narrow("htu,uhd->thd", dscores, key_tiles[position]) * scale
        dscore_list.append(dscores)
    parts = [
        key_terms(dscore_list[position], weight_list[position], queries, cotangent, scale)
        for position in range(SPAN + 1)
    ]
    outgoing = [
        jnp.stack(list(parts[SPAN - shift])).astype(jnp.bfloat16) for shift in range(1, SPAN + 1)
    ]
    place = lax.axis_index("ctx")
    need = min(-(-MAXDOC // tile), lax.axis_size("ctx"))
    near_states = [
        tile_state(
            key_tiles[position], value_tiles[position], doc_lengths, base - (SPAN - position) * tile
        )
        for position in range(SPAN)
    ]
    near_spans = [(place - SPAN + position, place - SPAN + position) for position in range(SPAN)]
    incoming = fold_states(near_states, front_flags(doc_lengths, near_spans, tile))
    covered = SPAN
    returned = None
    while covered < need:
        (flag,) = front_flags(doc_lengths, [(place - covered, place - 1)], tile)
        if 2 * covered >= need:
            incoming, outgoing = lax.optimization_barrier((incoming, outgoing))
            returned = [
                from_behind(outgoing[shift - 1], "ctx", -shift) for shift in range(1, SPAN + 1)
            ]
        incoming = incoming + (1.0 - flag) * send_state(incoming, "ctx", covered)
        covered *= 2
    linear_out = (
        narrow("htu,uhd->thd", attend, values)
        + wide("thd,hde->the", query_wide, incoming) * carried_prev[:, None, None]
    )
    weighted = cotangent.astype(jnp.float32) * gain[None]
    squares, projection = lax.psum(
        jnp.stack(
            [
                jnp.sum(linear_out * linear_out, axis=(1, 2)),
                jnp.sum(weighted * linear_out, axis=(1, 2)),
            ]
        ),
        "head",
    )
    inverse = lax.rsqrt(squares / features + norm_eps)
    mixed = (linear_out * inverse[:, None, None] * gain[None] + soft_out).astype(jnp.bfloat16)
    inner = (
        inverse[:, None, None] * weighted
        - linear_out * (inverse**3 * projection / features)[:, None, None]
    ).astype(jnp.bfloat16)
    inner_wide = inner.astype(jnp.float32)
    back = (narrow("thd,uhd->htu", inner, values) * same_tile).astype(jnp.bfloat16)
    query_linear = (
        narrow("htu,uhd->thd", back, keys)
        + wide("the,hde->thd", inner_wide, incoming) * carried_prev[:, None, None]
    )
    tile_sum = narrow(
        "thd,the->hde", jnp.where(keep_first, queries, jnp.zeros_like(queries)), inner
    )
    key_soft, value_soft = parts[SPAN]
    if returned is None:
        returned = [from_behind(outgoing[shift - 1], "ctx", -shift) for shift in range(1, SPAN + 1)]
    part = tile_sum
    covered = 1
    while 2 * covered < need:
        (flag,) = back_flags(doc_lengths, [(place, place + covered - 1)], tile)
        received = send_state(part, "ctx", -covered)
        if covered == 1:
            received, returned = lax.optimization_barrier((received, returned))
        part = part + (1.0 - flag) * received
        covered *= 2
    for moved in returned:
        key_soft = key_soft + moved[0].astype(jnp.float32)
        value_soft = value_soft + moved[1].astype(jnp.float32)
    later = send_state(part, "ctx", -1)
    if covered < need:
        (flag,) = back_flags(doc_lengths, [(place + 1, place + covered)], tile)
        later = later + (1.0 - flag) * send_state(part, "ctx", -1 - covered)
    key_linear = (
        narrow("htu,thd->uhd", back, queries)
        + wide("uhe,hde->uhd", values.astype(jnp.float32), later) * carried_next[:, None, None]
    )
    value_linear = (
        narrow("htu,the->uhe", attend, inner)
        + wide("uhd,hde->uhe", keys.astype(jnp.float32), later) * carried_next[:, None, None]
    )
    query_grad = (query_linear + query_soft).astype(jnp.bfloat16)
    key_grad = (key_linear + key_soft).astype(jnp.bfloat16)
    value_grad = (value_linear + value_soft).astype(jnp.bfloat16)
    return (mixed, query_grad, key_grad, value_grad)


def solution(mesh):
    placed = (
        P("ctx", "head", None),
        P("ctx", "head", None),
        P("ctx", "head", None),
        P("head", None),
        P(),
        P("ctx", "head", None),
    )
    return jax.shard_map(
        per_device,
        mesh=mesh,
        in_specs=placed,
        out_specs=(
            P("ctx", "head", None),
            P("ctx", "head", None),
            P("ctx", "head", None),
            P("ctx", "head", None),
        ),
        check_vma=False,
    )
```

profile of v0, /device:TPU:127, one launch (start us, length us, event | category | flops | bytes accessed | tf_op | source)
XLA Modules:
  0.0 135.6 jit_solution(5013973241469704528)
XLA Ops:
  0.6 1.1 copy_bitcast_fusion
  1.8 4.7 %collective-permute-start.1 = (bf16[2,128,8,128]{3,1,2,0:T(8,128)(2,1)S(1)}, bf16[2,128,8,128]{3,1,2,0:T(8,128)(2,1)S(1)}, u32[]{:S(2)}, u32[]{:S(2)}) collective-permute-start(bf16[2,128,8,128]{3,1,2,0:T(8,128)(2,1)S(1)} %pad_maximum_fusion), channel_id=1, source_target_pairs={{0,8},{4,12},{8,16},{12,20},{16,24},{20,28},{24,32},{28,36},{32,40... | collective-permute-start | bytes 1572872 | tf_op jit(solution)/shard_map/ppermute | solution.py:15
  6.5 4.0 %collective-permute-start = (bf16[2,128,8,128]{3,1,2,0:T(8,128)(2,1)S(1)}, bf16[2,128,8,128]{3,1,2,0:T(8,128)(2,1)S(1)}, u32[]{:S(2)}, u32[]{:S(2)}) collective-permute-start(bf16[2,128,8,128]{3,1,2,0:T(8,128)(2,1)S(1)} %pad_maximum_fusion), channel_id=1, source_target_pairs={{0,4},{4,8},{8,12},{12,16},{16,20},{20,24},{24,28},{28,32},{32,36}... | collective-permute-start | bytes 1572872 | tf_op jit(solution)/shard_map/ppermute | solution.py:15
  17.7 1.3 broadcast_compare_fusion.1
  35.1 3.1 %collective-permute-start.2 = (bf16[8,128,128]{2,1,0:T(8,128)(2,1)S(1)}, bf16[8,128,128]{2,1,0:T(8,128)(2,1)S(1)}, u32[]{:S(2)}, u32[]{:S(2)}) collective-permute-start(bf16[8,128,128]{2,1,0:T(8,128)(2,1)S(1)} %get-tuple-element.71), channel_id=1, source_target_pairs={{0,8},{4,12},{8,16},{12,20},{16,24},{20,28},{24,32},{28,36},{32,40... | collective-permute-start | bytes 786440 | tf_op jit(solution)/shard_map/ppermute | solution.py:15
  40.1 0.9 pad_maximum_fusion.2
  41.3 3.2 %collective-permute-done.2 = bf16[8,128,128]{2,1,0:T(8,128)(2,1)S(1)} collective-permute-done((bf16[8,128,128]{2,1,0:T(8,128)(2,1)S(1)}, bf16[8,128,128]{2,1,0:T(8,128)(2,1)S(1)}, u32[]{:S(2)}, u32[]{:S(2)}) %collective-permute-start.2) | collective-permute-done | bytes 262176 | tf_op jit(solution)/shard_map/ppermute | solution.py:15
  44.5 4.0 %collective-permute-start.3 = (bf16[8,128,128]{2,1,0:T(8,128)(2,1)S(1)}, bf16[8,128,128]{2,1,0:T(8,128)(2,1)S(1)}, u32[]{:S(2)}, u32[]{:S(2)}) collective-permute-start(bf16[8,128,128]{2,1,0:T(8,128)(2,1)S(1)} %fusion.54), channel_id=1, source_target_pairs={{0,16},{4,20},{8,24},{12,28},{16,32},{20,36},{24,40},{28,44},{32,4... | collective-permute-start | bytes 786440 | tf_op jit(solution)/shard_map/ppermute | solution.py:15
  48.6 0.9 pad_maximum_fusion.1
  49.8 6.0 %collective-permute-done.3 = bf16[8,128,128]{2,1,0:T(8,128)(2,1)S(1)} collective-permute-done((bf16[8,128,128]{2,1,0:T(8,128)(2,1)S(1)}, bf16[8,128,128]{2,1,0:T(8,128)(2,1)S(1)}, u32[]{:S(2)}, u32[]{:S(2)}) %collective-permute-start.3) | collective-permute-done | bytes 262176 | tf_op jit(solution)/shard_map/ppermute | solution.py:15
  55.9 2.6 %collective-permute-start.4 = (bf16[8,128,128]{2,1,0:T(8,128)(2,1)S(1)}, bf16[8,128,128]{2,1,0:T(8,128)(2,1)S(1)}, u32[]{:S(2)}, u32[]{:S(2)}) collective-permute-start(bf16[8,128,128]{2,1,0:T(8,128)(2,1)S(1)} %convert_element_type.228), channel_id=1, source_target_pairs={{0,32},{4,36},{8,40},{12,44},{16,48},{20,52},{24,56},{28,60},{32,6... | collective-permute-start | bytes 786440 | tf_op jit(solution)/shard_map/ppermute | solution.py:15
  58.5 1.1 fusion.14
  59.6 3.1 %collective-permute-start.6 = (bf16[2,128,8,128]{3,1,2,0:T(8,128)(2,1)}, bf16[2,128,8,128]{3,1,2,0:T(8,128)(2,1)}, u32[]{:S(2)}, u32[]{:S(2)}) collective-permute-start(bf16[2,128,8,128]{3,1,2,0:T(8,128)(2,1)} %pad_maximum_fusion.1), channel_id=1, source_target_pairs={{4,0},{8,4},{12,8},{16,12},{20,16},{24,20},{28,24},{32,28},{36,32}... | collective-permute-start | bytes 1572872 | tf_op jit(solution)/shard_map/ppermute | solution.py:15
  62.7 3.6 %collective-permute-start.7 = (bf16[2,128,8,128]{3,1,2,0:T(8,128)(2,1)}, bf16[2,128,8,128]{3,1,2,0:T(8,128)(2,1)}, u32[]{:S(2)}, u32[]{:S(2)}) collective-permute-start(bf16[2,128,8,128]{3,1,2,0:T(8,128)(2,1)} %pad_maximum_fusion.2), channel_id=1, source_target_pairs={{8,0},{12,4},{16,8},{20,12},{24,16},{28,20},{32,24},{36,28},{40,32... | collective-permute-start | bytes 1572872 | tf_op jit(solution)/shard_map/ppermute | solution.py:15
  67.5 5.8 %psum.7 = f32[2,128]{1,0:T(2,128)S(1)} all-reduce(f32[2,128]{1,0:T(2,128)S(1)} %pad_maximum_fusion.3), channel_id=1, replica_groups=mesh['ctx'=64,'head'=4] {'head'}, use_global_device_ids=true, to_apply=%region_18.19 | all-reduce | flops 256 | bytes 2048 | tf_op jit(solution)/shard_map/psum | solution.py:169
  73.9 4.6 %collective-permute-start.5 = (bf16[8,128,128]{2,1,0:T(8,128)(2,1)S(1)}, bf16[8,128,128]{2,1,0:T(8,128)(2,1)S(1)}, u32[]{:S(2)}, u32[]{:S(2)}) collective-permute-start(bf16[8,128,128]{2,1,0:T(8,128)(2,1)S(1)} %get-tuple-element.82), channel_id=1, source_target_pairs={{4,0},{8,4},{12,8},{16,12},{20,16},{24,20},{28,24},{32,28},{36,32}... | collective-permute-start | bytes 786440 | tf_op jit(solution)/shard_map/ppermute | solution.py:15
  79.1 10.4 %collective-permute-done.5 = bf16[8,128,128]{2,1,0:T(8,128)(2,1)S(1)} collective-permute-done((bf16[8,128,128]{2,1,0:T(8,128)(2,1)S(1)}, bf16[8,128,128]{2,1,0:T(8,128)(2,1)S(1)}, u32[]{:S(2)}, u32[]{:S(2)}) %collective-permute-start.5) | collective-permute-done | bytes 262176 | tf_op jit(solution)/shard_map/ppermute | solution.py:15
  89.6 1.9 %collective-permute-start.8 = (bf16[8,128,128]{2,1,0:T(8,128)(2,1)S(1)}, bf16[8,128,128]{2,1,0:T(8,128)(2,1)S(1)}, u32[]{:S(2)}, u32[]{:S(2)}) collective-permute-start(bf16[8,128,128]{2,1,0:T(8,128)(2,1)S(1)} %get-tuple-element.45), channel_id=1, source_target_pairs={{8,0},{12,4},{16,8},{20,12},{24,16},{28,20},{32,24},{36,28},{40,32... | collective-permute-start | bytes 786440 | tf_op jit(solution)/shard_map/ppermute | solution.py:15
  92.3 8.9 %collective-permute-done.8 = bf16[8,128,128]{2,1,0:T(8,128)(2,1)S(1)} collective-permute-done((bf16[8,128,128]{2,1,0:T(8,128)(2,1)S(1)}, bf16[8,128,128]{2,1,0:T(8,128)(2,1)S(1)}, u32[]{:S(2)}, u32[]{:S(2)}) %collective-permute-start.8) | collective-permute-done | bytes 262176 | tf_op jit(solution)/shard_map/ppermute | solution.py:15
  101.2 1.9 %collective-permute-start.9 = (bf16[8,128,128]{2,1,0:T(8,128)(2,1)S(1)}, bf16[8,128,128]{2,1,0:T(8,128)(2,1)S(1)}, u32[]{:S(2)}, u32[]{:S(2)}) collective-permute-start(bf16[8,128,128]{2,1,0:T(8,128)(2,1)S(1)} %fusion.55), channel_id=1, source_target_pairs={{16,0},{20,4},{24,8},{28,12},{32,16},{36,20},{40,24},{44,28},{48,3... | collective-permute-start | bytes 786440 | tf_op jit(solution)/shard_map/ppermute | solution.py:15
  103.4 10.7 %collective-permute-done.9 = bf16[8,128,128]{2,1,0:T(8,128)(2,1)S(1)} collective-permute-done((bf16[8,128,128]{2,1,0:T(8,128)(2,1)S(1)}, bf16[8,128,128]{2,1,0:T(8,128)(2,1)S(1)}, u32[]{:S(2)}, u32[]{:S(2)}) %collective-permute-start.9) | collective-permute-done | bytes 262176 | tf_op jit(solution)/shard_map/ppermute | solution.py:15
  114.3 1.9 %collective-permute-start.11 = (bf16[8,128,128]{2,1,0:T(8,128)(2,1)S(1)}, bf16[8,128,128]{2,1,0:T(8,128)(2,1)S(1)}, u32[]{:S(2)}, u32[]{:S(2)}) collective-permute-start(bf16[8,128,128]{2,1,0:T(8,128)(2,1)S(1)} %add_convert_fusion), channel_id=1, source_target_pairs={{36,0},{40,4},{44,8},{48,12},{52,16},{56,20},{60,24},{64,28},{68,3... | collective-permute-start | bytes 786440 | tf_op jit(solution)/shard_map/ppermute | solution.py:15
  116.2 2.2 %collective-permute-start.10 = (bf16[8,128,128]{2,1,0:T(8,128)(2,1)S(1)}, bf16[8,128,128]{2,1,0:T(8,128)(2,1)S(1)}, u32[]{:S(2)}, u32[]{:S(2)}) collective-permute-start(bf16[8,128,128]{2,1,0:T(8,128)(2,1)S(1)} %add_convert_fusion), channel_id=1, source_target_pairs={{4,0},{8,4},{12,8},{16,12},{20,16},{24,20},{28,24},{32,28},{36,32}... | collective-permute-start | bytes 786440 | tf_op jit(solution)/shard_map/ppermute | solution.py:15
  118.6 0.9 copy.204
  119.5 0.9 copy.205
  120.6 6.8 %collective-permute-done.11 = bf16[8,128,128]{2,1,0:T(8,128)(2,1)S(1)} collective-permute-done((bf16[8,128,128]{2,1,0:T(8,128)(2,1)S(1)}, bf16[8,128,128]{2,1,0:T(8,128)(2,1)S(1)}, u32[]{:S(2)}, u32[]{:S(2)}) %collective-permute-start.11) | collective-permute-done | bytes 262176 | tf_op jit(solution)/shard_map/ppermute | solution.py:15
  127.4 2.6 %collective-permute-done.10 = bf16[8,128,128]{2,1,0:T(8,128)(2,1)S(1)} collective-permute-done((bf16[8,128,128]{2,1,0:T(8,128)(2,1)S(1)}, bf16[8,128,128]{2,1,0:T(8,128)(2,1)S(1)}, u32[]{:S(2)}, u32[]{:S(2)}) %collective-permute-start.10) | collective-permute-done | bytes 262176 | tf_op jit(solution)/shard_map/ppermute | solution.py:15
  130.5 1.3 fusion.31
  131.8 0.7 fusion.28
  132.5 1.3 fusion.35
  133.8 0.9 copy.206
  134.7 0.9 copy.207
  (103 shorter events, 19.5 us)
Async XLA Ops:
  1.8 8.8 %copy-start.8 = (s32[64]{0:T(128)S(1)}, s32[64]{0:T(128)}, u32[]{:S(2)}) copy-start(s32[64]{0:T(128)} %param.10) | copy-start | bytes 772
  1.8 29.5 %collective-permute-start.1 = (bf16[2,128,8,128]{3,1,2,0:T(8,128)(2,1)S(1)}, bf16[2,128,8,128]{3,1,2,0:T(8,128)(2,1)S(1)}, u32[]{:S(2)}, u32[]{:S(2)}) collective-permute-start(bf16[2,128,8,128]{3,1,2,0:T(8,128)(2,1)S(1)} %pad_maximum_fusion), channel_id=1, source_target_pairs={{0,8},{4,12},{8,16},{12,20},{16,24},{20,28},{24,32},{28,36},{32,40... | collective-permute-start | bytes 1572872 | tf_op jit(solution)/shard_map/ppermute | solution.py:15
  6.5 25.1 %collective-permute-start = (bf16[2,128,8,128]{3,1,2,0:T(8,128)(2,1)S(1)}, bf16[2,128,8,128]{3,1,2,0:T(8,128)(2,1)S(1)}, u32[]{:S(2)}, u32[]{:S(2)}) collective-permute-start(bf16[2,128,8,128]{3,1,2,0:T(8,128)(2,1)S(1)} %pad_maximum_fusion), channel_id=1, source_target_pairs={{0,4},{4,8},{8,12},{12,16},{16,20},{20,24},{24,28},{28,32},{32,36}... | collective-permute-start | bytes 1572872 | tf_op jit(solution)/shard_map/ppermute | solution.py:15
  10.5 20.5 %copy-start.3 = (bf16[128,8,128]{2,1,0:T(8,128)(2,1)S(1)}, bf16[128,8,128]{2,1,0:T(8,128)(2,1)}, u32[]{:S(2)}) copy-start(bf16[128,8,128]{2,1,0:T(8,128)(2,1)} %param.7) | copy-start | bytes 786436
  10.5 20.5 %copy-start.1 = (bf16[128,8,128]{2,1,0:T(8,128)(2,1)S(1)}, bf16[128,8,128]{2,1,0:T(8,128)(2,1)}, u32[]{:S(2)}) copy-start(bf16[128,8,128]{2,1,0:T(8,128)(2,1)} %param.6) | copy-start | bytes 786436
  32.0 1.0 copy-start
  33.2 1.0 copy-start.2
  35.1 9.3 %collective-permute-start.2 = (bf16[8,128,128]{2,1,0:T(8,128)(2,1)S(1)}, bf16[8,128,128]{2,1,0:T(8,128)(2,1)S(1)}, u32[]{:S(2)}, u32[]{:S(2)}) collective-permute-start(bf16[8,128,128]{2,1,0:T(8,128)(2,1)S(1)} %get-tuple-element.71), channel_id=1, source_target_pairs={{0,8},{4,12},{8,16},{12,20},{16,24},{20,28},{24,32},{28,36},{32,40... | collective-permute-start | bytes 786440 | tf_op jit(solution)/shard_map/ppermute | solution.py:15
  44.5 11.2 %collective-permute-start.3 = (bf16[8,128,128]{2,1,0:T(8,128)(2,1)S(1)}, bf16[8,128,128]{2,1,0:T(8,128)(2,1)S(1)}, u32[]{:S(2)}, u32[]{:S(2)}) collective-permute-start(bf16[8,128,128]{2,1,0:T(8,128)(2,1)S(1)} %fusion.54), channel_id=1, source_target_pairs={{0,16},{4,20},{8,24},{12,28},{16,32},{20,36},{24,40},{28,44},{32,4... | collective-permute-start | bytes 786440 | tf_op jit(solution)/shard_map/ppermute | solution.py:15
  55.9 10.5 %collective-permute-start.4 = (bf16[8,128,128]{2,1,0:T(8,128)(2,1)S(1)}, bf16[8,128,128]{2,1,0:T(8,128)(2,1)S(1)}, u32[]{:S(2)}, u32[]{:S(2)}) collective-permute-start(bf16[8,128,128]{2,1,0:T(8,128)(2,1)S(1)} %convert_element_type.228), channel_id=1, source_target_pairs={{0,32},{4,36},{8,40},{12,44},{16,48},{20,52},{24,56},{28,60},{32,6... | collective-permute-start | bytes 786440 | tf_op jit(solution)/shard_map/ppermute | solution.py:15
  59.6 29.9 %collective-permute-start.6 = (bf16[2,128,8,128]{3,1,2,0:T(8,128)(2,1)}, bf16[2,128,8,128]{3,1,2,0:T(8,128)(2,1)}, u32[]{:S(2)}, u32[]{:S(2)}) collective-permute-start(bf16[2,128,8,128]{3,1,2,0:T(8,128)(2,1)} %pad_maximum_fusion.1), channel_id=1, source_target_pairs={{4,0},{8,4},{12,8},{16,12},{20,16},{24,20},{28,24},{32,28},{36,32}... | collective-permute-start | bytes 1572872 | tf_op jit(solution)/shard_map/ppermute | solution.py:15
  62.7 26.8 %collective-permute-start.7 = (bf16[2,128,8,128]{3,1,2,0:T(8,128)(2,1)}, bf16[2,128,8,128]{3,1,2,0:T(8,128)(2,1)}, u32[]{:S(2)}, u32[]{:S(2)}) collective-permute-start(bf16[2,128,8,128]{3,1,2,0:T(8,128)(2,1)} %pad_maximum_fusion.2), channel_id=1, source_target_pairs={{8,0},{12,4},{16,8},{20,12},{24,16},{28,20},{32,24},{36,28},{40,32... | collective-permute-start | bytes 1572872 | tf_op jit(solution)/shard_map/ppermute | solution.py:15
  66.4 0.7 copy-start.5
  66.4 0.7 copy-start.7
  73.5 5.0 %copy-start.4 = (f32[128,8,128]{2,0,1:T(8,128)S(1)}, f32[128,8,128]{2,0,1:T(8,128)}, u32[]{:S(2)}) copy-start(f32[128,8,128]{2,0,1:T(8,128)} %fusion.14) | copy-start | bytes 1572868
  73.9 15.6 %collective-permute-start.5 = (bf16[8,128,128]{2,1,0:T(8,128)(2,1)S(1)}, bf16[8,128,128]{2,1,0:T(8,128)(2,1)S(1)}, u32[]{:S(2)}, u32[]{:S(2)}) collective-permute-start(bf16[8,128,128]{2,1,0:T(8,128)(2,1)S(1)} %get-tuple-element.82), channel_id=1, source_target_pairs={{4,0},{8,4},{12,8},{16,12},{20,16},{24,20},{28,24},{32,28},{36,32}... | collective-permute-start | bytes 786440 | tf_op jit(solution)/shard_map/ppermute | solution.py:15
  89.5 2.0 %copy-start.6 = (bf16[8,128,128]{2,1,0:T(8,128)(2,1)S(1)}, bf16[8,128,128]{2,1,0:T(8,128)(2,1)}, u32[]{:S(2)}) copy-start(bf16[8,128,128]{2,1,0:T(8,128)(2,1)} %copy-done.5) | copy-start | bytes 786436
  89.6 11.5 %collective-permute-start.8 = (bf16[8,128,128]{2,1,0:T(8,128)(2,1)S(1)}, bf16[8,128,128]{2,1,0:T(8,128)(2,1)S(1)}, u32[]{:S(2)}, u32[]{:S(2)}) collective-permute-start(bf16[8,128,128]{2,1,0:T(8,128)(2,1)S(1)} %get-tuple-element.45), channel_id=1, source_target_pairs={{8,0},{12,4},{16,8},{20,12},{24,16},{28,20},{32,24},{36,28},{40,32... | collective-permute-start | bytes 786440 | tf_op jit(solution)/shard_map/ppermute | solution.py:15
  101.2 12.9 %collective-permute-start.9 = (bf16[8,128,128]{2,1,0:T(8,128)(2,1)S(1)}, bf16[8,128,128]{2,1,0:T(8,128)(2,1)S(1)}, u32[]{:S(2)}, u32[]{:S(2)}) collective-permute-start(bf16[8,128,128]{2,1,0:T(8,128)(2,1)S(1)} %fusion.55), channel_id=1, source_target_pairs={{16,0},{20,4},{24,8},{28,12},{32,16},{36,20},{40,24},{44,28},{48,3... | collective-permute-start | bytes 786440 | tf_op jit(solution)/shard_map/ppermute | solution.py:15
  114.3 13.1 %collective-permute-start.11 = (bf16[8,128,128]{2,1,0:T(8,128)(2,1)S(1)}, bf16[8,128,128]{2,1,0:T(8,128)(2,1)S(1)}, u32[]{:S(2)}, u32[]{:S(2)}) collective-permute-start(bf16[8,128,128]{2,1,0:T(8,128)(2,1)S(1)} %add_convert_fusion), channel_id=1, source_target_pairs={{36,0},{40,4},{44,8},{48,12},{52,16},{56,20},{60,24},{64,28},{68,3... | collective-permute-start | bytes 786440 | tf_op jit(solution)/shard_map/ppermute | solution.py:15
  116.2 13.8 %collective-permute-start.10 = (bf16[8,128,128]{2,1,0:T(8,128)(2,1)S(1)}, bf16[8,128,128]{2,1,0:T(8,128)(2,1)S(1)}, u32[]{:S(2)}, u32[]{:S(2)}) collective-permute-start(bf16[8,128,128]{2,1,0:T(8,128)(2,1)S(1)} %add_convert_fusion), channel_id=1, source_target_pairs={{4,0},{8,4},{12,8},{16,12},{20,16},{24,20},{28,24},{32,28},{36,32}... | collective-permute-start | bytes 786440 | tf_op jit(solution)/shard_map/ppermute | solution.py:15
where the time goes:
time: 136 us
  waiting for transfers between devices  48.6 us (36%)
  starting transfers between devices  37.7 us (28%)
  matrix products  12.8 us (9%)
  local copies, waits for them, and re-layouts  12.4 us (9%)
  between operations  12 us (9%)
  other arithmetic  6.32 us (5%)
  blocking collectives  5.76 us (4%)
    ppermute x12, waiting for transfers between devices, from_behind(): return lax.ppermute(x, axis, pairs)  48.6 us
    ppermute x12, starting transfers between devices, from_behind(): return lax.ppermute(x, axis, pairs)  37.7 us
    dot_general x26, matrix products, narrow(): return jnp.einsum(form, left, right, preferred_element_type=jnp.float32)  10.5 us
    psum x1, blocking collectives, per_device(): lax.psum(jnp.stack([jnp.sum(linear_out * linear_out, axis=(1, 2)), jnp.su...  5.76 us
    unnamed x22, local copies, waits for them, and re-layouts  5.14 us
  transfers between devices with their start and end apart: 12, of which 7 were waited for; matrix products, arithmetic and copies ran while one was open for 15% of the time, Pallas kernels for 0%

commit v1 on v0

--- a/solution.py
+++ b/solution.py
@@ -2,6 +2,7 @@
 import jax.numpy as jnp
 from jax import lax
 from jax.sharding import PartitionSpec as P
+from jax.lax import all_gather
 
 SPAN = 2
 MAXDOC = 2048
@@ -166,14 +167,14 @@
         + wide("thd,hde->the", query_wide, incoming) * carried_prev[:, None, None]
     )
     weighted = cotangent.astype(jnp.float32) * gain[None]
-    squares, projection = lax.psum(
+    handle_spots = lambda sheet: all_gather(sheet, axis_name="head").sum(axis=0)
+    squares, projection = handle_spots(
         jnp.stack(
             [
                 jnp.sum(linear_out * linear_out, axis=(1, 2)),
                 jnp.sum(weighted * linear_out, axis=(1, 2)),
             ]
-        ),
-        "head",
+        )
     )
     inverse = lax.rsqrt(squares / features + norm_eps)
     mixed = (linear_out * inverse[:, None, None] * gain[None] + soft_out).astype(jnp.bfloat16)

time: 136 us -> 136 us (level)
    psum x1 -> x0, blocking collectives: 5.76 us -> none  [per_device(): lax.psum(jnp.stack([jnp.sum(linear_out * linear_out, axis=(1, 2)), jnp.su...]
    all_gather x0 -> x1, blocking collectives: none -> 5 us  [per_device(): handle_spots = lambda sheet: all_gather(sheet, axis_name='head').sum(axis=0)]
where the time goes in v1:
time: 136 us
  waiting for transfers between devices  49.2 us (36%)
  starting transfers between devices  37.8 us (28%)
  matrix products  12.8 us (9%)
  local copies, waits for them, and re-layouts  12.4 us (9%)
  between operations  12 us (9%)
  other arithmetic  6.34 us (5%)
  blocking collectives  5 us (4%)
    ppermute x12, waiting for transfers between devices, from_behind(): return lax.ppermute(x, axis, pairs)  49.2 us
    ppermute x12, starting transfers between devices, from_behind(): return lax.ppermute(x, axis, pairs)  37.8 us
    dot_general x26, matrix products, narrow(): return jnp.einsum(form, left, right, preferred_element_type=jnp.float32)  10.5 us
    unnamed x22, local copies, waits for them, and re-layouts  5.14 us
    all_gather x1, blocking collectives, per_device(): handle_spots = lambda sheet: all_gather(sheet, axis_name='head').sum(axis=0)  5 us
  transfers between devices with their start and end apart: 12, of which 7 were waited for; matrix products, arithmetic and copies ran while one was open for 15% of the time, Pallas kernels for 0%

profile of v1, /device:TPU:127, one launch (start us, length us, event | category | flops | bytes accessed | tf_op | source)
XLA Modules:
  0.0 135.6 jit_solution(17215246734839516701)
XLA Ops:
  0.6 1.1 copy_bitcast_fusion
  1.8 4.7 %collective-permute-start.1 = (bf16[2,128,8,128]{3,1,2,0:T(8,128)(2,1)S(1)}, bf16[2,128,8,128]{3,1,2,0:T(8,128)(2,1)S(1)}, u32[]{:S(2)}, u32[]{:S(2)}) collective-permute-start(bf16[2,128,8,128]{3,1,2,0:T(8,128)(2,1)S(1)} %pad_maximum_fusion), channel_id=1, source_target_pairs={{0,8},{4,12},{8,16},{12,20},{16,24},{20,28},{24,32},{28,36},{32,40... | collective-permute-start | bytes 1572872 | tf_op jit(solution)/shard_map/ppermute | solution.py:16
  6.5 4.0 %collective-permute-start = (bf16[2,128,8,128]{3,1,2,0:T(8,128)(2,1)S(1)}, bf16[2,128,8,128]{3,1,2,0:T(8,128)(2,1)S(1)}, u32[]{:S(2)}, u32[]{:S(2)}) collective-permute-start(bf16[2,128,8,128]{3,1,2,0:T(8,128)(2,1)S(1)} %pad_maximum_fusion), channel_id=1, source_target_pairs={{0,4},{4,8},{8,12},{12,16},{16,20},{20,24},{24,28},{28,32},{32,36}... | collective-permute-start | bytes 1572872 | tf_op jit(solution)/shard_map/ppermute | solution.py:16
  17.7 1.3 broadcast_compare_fusion.1
  35.1 3.1 %collective-permute-start.2 = (bf16[8,128,128]{2,1,0:T(8,128)(2,1)S(1)}, bf16[8,128,128]{2,1,0:T(8,128)(2,1)S(1)}, u32[]{:S(2)}, u32[]{:S(2)}) collective-permute-start(bf16[8,128,128]{2,1,0:T(8,128)(2,1)S(1)} %get-tuple-element.75), channel_id=1, source_target_pairs={{0,8},{4,12},{8,16},{12,20},{16,24},{20,28},{24,32},{28,36},{32,40... | collective-permute-start | bytes 786440 | tf_op jit(solution)/shard_map/ppermute | solution.py:16
  40.1 0.9 pad_maximum_fusion.2
  41.3 3.2 %collective-permute-done.2 = bf16[8,128,128]{2,1,0:T(8,128)(2,1)S(1)} collective-permute-done((bf16[8,128,128]{2,1,0:T(8,128)(2,1)S(1)}, bf16[8,128,128]{2,1,0:T(8,128)(2,1)S(1)}, u32[]{:S(2)}, u32[]{:S(2)}) %collective-permute-start.2) | collective-permute-done | bytes 262176 | tf_op jit(solution)/shard_map/ppermute | solution.py:16
  44.5 4.0 %collective-permute-start.3 = (bf16[8,128,128]{2,1,0:T(8,128)(2,1)S(1)}, bf16[8,128,128]{2,1,0:T(8,128)(2,1)S(1)}, u32[]{:S(2)}, u32[]{:S(2)}) collective-permute-start(bf16[8,128,128]{2,1,0:T(8,128)(2,1)S(1)} %fusion.54), channel_id=1, source_target_pairs={{0,16},{4,20},{8,24},{12,28},{16,32},{20,36},{24,40},{28,44},{32,4... | collective-permute-start | bytes 786440 | tf_op jit(solution)/shard_map/ppermute | solution.py:16
  48.6 0.9 pad_maximum_fusion.1
  49.8 6.0 %collective-permute-done.3 = bf16[8,128,128]{2,1,0:T(8,128)(2,1)S(1)} collective-permute-done((bf16[8,128,128]{2,1,0:T(8,128)(2,1)S(1)}, bf16[8,128,128]{2,1,0:T(8,128)(2,1)S(1)}, u32[]{:S(2)}, u32[]{:S(2)}) %collective-permute-start.3) | collective-permute-done | bytes 262176 | tf_op jit(solution)/shard_map/ppermute | solution.py:16
  55.9 2.6 %collective-permute-start.4 = (bf16[8,128,128]{2,1,0:T(8,128)(2,1)S(1)}, bf16[8,128,128]{2,1,0:T(8,128)(2,1)S(1)}, u32[]{:S(2)}, u32[]{:S(2)}) collective-permute-start(bf16[8,128,128]{2,1,0:T(8,128)(2,1)S(1)} %convert_element_type.228), channel_id=1, source_target_pairs={{0,32},{4,36},{8,40},{12,44},{16,48},{20,52},{24,56},{28,60},{32,6... | collective-permute-start | bytes 786440 | tf_op jit(solution)/shard_map/ppermute | solution.py:16
  58.5 1.1 fusion.14
  59.6 3.1 %collective-permute-start.6 = (bf16[2,128,8,128]{3,1,2,0:T(8,128)(2,1)}, bf16[2,128,8,128]{3,1,2,0:T(8,128)(2,1)}, u32[]{:S(2)}, u32[]{:S(2)}) collective-permute-start(bf16[2,128,8,128]{3,1,2,0:T(8,128)(2,1)} %pad_maximum_fusion.1), channel_id=1, source_target_pairs={{4,0},{8,4},{12,8},{16,12},{20,16},{24,20},{28,24},{32,28},{36,32}... | collective-permute-start | bytes 1572872 | tf_op jit(solution)/shard_map/ppermute | solution.py:16
  62.7 3.6 %collective-permute-start.7 = (bf16[2,128,8,128]{3,1,2,0:T(8,128)(2,1)}, bf16[2,128,8,128]{3,1,2,0:T(8,128)(2,1)}, u32[]{:S(2)}, u32[]{:S(2)}) collective-permute-start(bf16[2,128,8,128]{3,1,2,0:T(8,128)(2,1)} %pad_maximum_fusion.2), channel_id=1, source_target_pairs={{8,0},{12,4},{16,8},{20,12},{24,16},{28,20},{32,24},{36,28},{40,32... | collective-permute-start | bytes 1572872 | tf_op jit(solution)/shard_map/ppermute | solution.py:16
  67.5 5.0 %all-gather.1 = f32[4,2,128]{2,1,0:T(2,128)S(1)} all-gather(f32[1,2,128]{2,1,0:T(2,128)S(1)} %maximum_bitcast_fusion), channel_id=2, replica_groups=mesh['ctx'=64,'head'=4] {'head'}, dimensions={0}, use_global_device_ids=true | all-gather | bytes 5120 | tf_op jit(solution)/shard_map/all_gather | solution.py:170
  73.2 4.6 %collective-permute-start.5 = (bf16[8,128,128]{2,1,0:T(8,128)(2,1)S(1)}, bf16[8,128,128]{2,1,0:T(8,128)(2,1)S(1)}, u32[]{:S(2)}, u32[]{:S(2)}) collective-permute-start(bf16[8,128,128]{2,1,0:T(8,128)(2,1)S(1)} %get-tuple-element.86), channel_id=1, source_target_pairs={{4,0},{8,4},{12,8},{16,12},{20,16},{24,20},{28,24},{32,28},{36,32}... | collective-permute-start | bytes 786440 | tf_op jit(solution)/shard_map/ppermute | solution.py:16
  78.4 11.0 %collective-permute-done.5 = bf16[8,128,128]{2,1,0:T(8,128)(2,1)S(1)} collective-permute-done((bf16[8,128,128]{2,1,0:T(8,128)(2,1)S(1)}, bf16[8,128,128]{2,1,0:T(8,128)(2,1)S(1)}, u32[]{:S(2)}, u32[]{:S(2)}) %collective-permute-start.5) | collective-permute-done | bytes 262176 | tf_op jit(solution)/shard_map/ppermute | solution.py:16
  89.5 1.9 %collective-permute-start.8 = (bf16[8,128,128]{2,1,0:T(8,128)(2,1)S(1)}, bf16[8,128,128]{2,1,0:T(8,128)(2,1)S(1)}, u32[]{:S(2)}, u32[]{:S(2)}) collective-permute-start(bf16[8,128,128]{2,1,0:T(8,128)(2,1)S(1)} %get-tuple-element.49), channel_id=1, source_target_pairs={{8,0},{12,4},{16,8},{20,12},{24,16},{28,20},{32,24},{36,28},{40,32... | collective-permute-start | bytes 786440 | tf_op jit(solution)/shard_map/ppermute | solution.py:16
  92.2 9.0 %collective-permute-done.8 = bf16[8,128,128]{2,1,0:T(8,128)(2,1)S(1)} collective-permute-done((bf16[8,128,128]{2,1,0:T(8,128)(2,1)S(1)}, bf16[8,128,128]{2,1,0:T(8,128)(2,1)S(1)}, u32[]{:S(2)}, u32[]{:S(2)}) %collective-permute-start.8) | collective-permute-done | bytes 262176 | tf_op jit(solution)/shard_map/ppermute | solution.py:16
  101.2 1.9 %collective-permute-start.9 = (bf16[8,128,128]{2,1,0:T(8,128)(2,1)S(1)}, bf16[8,128,128]{2,1,0:T(8,128)(2,1)S(1)}, u32[]{:S(2)}, u32[]{:S(2)}) collective-permute-start(bf16[8,128,128]{2,1,0:T(8,128)(2,1)S(1)} %fusion.55), channel_id=1, source_target_pairs={{16,0},{20,4},{24,8},{28,12},{32,16},{36,20},{40,24},{44,28},{48,3... | collective-permute-start | bytes 786440 | tf_op jit(solution)/shard_map/ppermute | solution.py:16
  103.4 10.8 %collective-permute-done.9 = bf16[8,128,128]{2,1,0:T(8,128)(2,1)S(1)} collective-permute-done((bf16[8,128,128]{2,1,0:T(8,128)(2,1)S(1)}, bf16[8,128,128]{2,1,0:T(8,128)(2,1)S(1)}, u32[]{:S(2)}, u32[]{:S(2)}) %collective-permute-start.9) | collective-permute-done | bytes 262176 | tf_op jit(solution)/shard_map/ppermute | solution.py:16
  114.4 1.9 %collective-permute-start.11 = (bf16[8,128,128]{2,1,0:T(8,128)(2,1)S(1)}, bf16[8,128,128]{2,1,0:T(8,128)(2,1)S(1)}, u32[]{:S(2)}, u32[]{:S(2)}) collective-permute-start(bf16[8,128,128]{2,1,0:T(8,128)(2,1)S(1)} %add_convert_fusion), channel_id=1, source_target_pairs={{36,0},{40,4},{44,8},{48,12},{52,16},{56,20},{60,24},{64,28},{68,3... | collective-permute-start | bytes 786440 | tf_op jit(solution)/shard_map/ppermute | solution.py:16
  116.3 2.3 %collective-permute-start.10 = (bf16[8,128,128]{2,1,0:T(8,128)(2,1)S(1)}, bf16[8,128,128]{2,1,0:T(8,128)(2,1)S(1)}, u32[]{:S(2)}, u32[]{:S(2)}) collective-permute-start(bf16[8,128,128]{2,1,0:T(8,128)(2,1)S(1)} %add_convert_fusion), channel_id=1, source_target_pairs={{4,0},{8,4},{12,8},{16,12},{20,16},{24,20},{28,24},{32,28},{36,32}... | collective-permute-start | bytes 786440 | tf_op jit(solution)/shard_map/ppermute | solution.py:16
  118.8 0.9 copy.270
  119.7 0.9 copy.271
  120.8 6.5 %collective-permute-done.11 = bf16[8,128,128]{2,1,0:T(8,128)(2,1)S(1)} collective-permute-done((bf16[8,128,128]{2,1,0:T(8,128)(2,1)S(1)}, bf16[8,128,128]{2,1,0:T(8,128)(2,1)S(1)}, u32[]{:S(2)}, u32[]{:S(2)}) %collective-permute-start.11) | collective-permute-done | bytes 262176 | tf_op jit(solution)/shard_map/ppermute | solution.py:16
  127.3 2.7 %collective-permute-done.10 = bf16[8,128,128]{2,1,0:T(8,128)(2,1)S(1)} collective-permute-done((bf16[8,128,128]{2,1,0:T(8,128)(2,1)S(1)}, bf16[8,128,128]{2,1,0:T(8,128)(2,1)S(1)}, u32[]{:S(2)}, u32[]{:S(2)}) %collective-permute-start.10) | collective-permute-done | bytes 262176 | tf_op jit(solution)/shard_map/ppermute | solution.py:16
  130.5 1.3 fusion.31
  131.8 0.7 fusion.28
  132.5 1.3 fusion.35
  133.9 0.9 copy.272
  134.7 0.9 copy.273
  (104 shorter events, 19.5 us)
Async XLA Ops:
  1.8 8.8 %copy-start.8 = (s32[64]{0:T(128)S(1)}, s32[64]{0:T(128)}, u32[]{:S(2)}) copy-start(s32[64]{0:T(128)} %param.10) | copy-start | bytes 772
  1.8 29.5 %collective-permute-start.1 = (bf16[2,128,8,128]{3,1,2,0:T(8,128)(2,1)S(1)}, bf16[2,128,8,128]{3,1,2,0:T(8,128)(2,1)S(1)}, u32[]{:S(2)}, u32[]{:S(2)}) collective-permute-start(bf16[2,128,8,128]{3,1,2,0:T(8,128)(2,1)S(1)} %pad_maximum_fusion), channel_id=1, source_target_pairs={{0,8},{4,12},{8,16},{12,20},{16,24},{20,28},{24,32},{28,36},{32,40... | collective-permute-start | bytes 1572872 | tf_op jit(solution)/shard_map/ppermute | solution.py:16
  6.5 25.1 %collective-permute-start = (bf16[2,128,8,128]{3,1,2,0:T(8,128)(2,1)S(1)}, bf16[2,128,8,128]{3,1,2,0:T(8,128)(2,1)S(1)}, u32[]{:S(2)}, u32[]{:S(2)}) collective-permute-start(bf16[2,128,8,128]{3,1,2,0:T(8,128)(2,1)S(1)} %pad_maximum_fusion), channel_id=1, source_target_pairs={{0,4},{4,8},{8,12},{12,16},{16,20},{20,24},{24,28},{28,32},{32,36}... | collective-permute-start | bytes 1572872 | tf_op jit(solution)/shard_map/ppermute | solution.py:16
  10.5 20.5 %copy-start.3 = (bf16[128,8,128]{2,1,0:T(8,128)(2,1)S(1)}, bf16[128,8,128]{2,1,0:T(8,128)(2,1)}, u32[]{:S(2)}) copy-start(bf16[128,8,128]{2,1,0:T(8,128)(2,1)} %param.7) | copy-start | bytes 786436
  10.5 20.5 %copy-start.1 = (bf16[128,8,128]{2,1,0:T(8,128)(2,1)S(1)}, bf16[128,8,128]{2,1,0:T(8,128)(2,1)}, u32[]{:S(2)}) copy-start(bf16[128,8,128]{2,1,0:T(8,128)(2,1)} %param.6) | copy-start | bytes 786436
  32.0 1.0 copy-start
  33.2 1.0 copy-start.2
  35.1 9.3 %collective-permute-start.2 = (bf16[8,128,128]{2,1,0:T(8,128)(2,1)S(1)}, bf16[8,128,128]{2,1,0:T(8,128)(2,1)S(1)}, u32[]{:S(2)}, u32[]{:S(2)}) collective-permute-start(bf16[8,128,128]{2,1,0:T(8,128)(2,1)S(1)} %get-tuple-element.75), channel_id=1, source_target_pairs={{0,8},{4,12},{8,16},{12,20},{16,24},{20,28},{24,32},{28,36},{32,40... | collective-permute-start | bytes 786440 | tf_op jit(solution)/shard_map/ppermute | solution.py:16
  44.5 11.2 %collective-permute-start.3 = (bf16[8,128,128]{2,1,0:T(8,128)(2,1)S(1)}, bf16[8,128,128]{2,1,0:T(8,128)(2,1)S(1)}, u32[]{:S(2)}, u32[]{:S(2)}) collective-permute-start(bf16[8,128,128]{2,1,0:T(8,128)(2,1)S(1)} %fusion.54), channel_id=1, source_target_pairs={{0,16},{4,20},{8,24},{12,28},{16,32},{20,36},{24,40},{28,44},{32,4... | collective-permute-start | bytes 786440 | tf_op jit(solution)/shard_map/ppermute | solution.py:16
  55.9 10.5 %collective-permute-start.4 = (bf16[8,128,128]{2,1,0:T(8,128)(2,1)S(1)}, bf16[8,128,128]{2,1,0:T(8,128)(2,1)S(1)}, u32[]{:S(2)}, u32[]{:S(2)}) collective-permute-start(bf16[8,128,128]{2,1,0:T(8,128)(2,1)S(1)} %convert_element_type.228), channel_id=1, source_target_pairs={{0,32},{4,36},{8,40},{12,44},{16,48},{20,52},{24,56},{28,60},{32,6... | collective-permute-start | bytes 786440 | tf_op jit(solution)/shard_map/ppermute | solution.py:16
  59.6 29.8 %collective-permute-start.6 = (bf16[2,128,8,128]{3,1,2,0:T(8,128)(2,1)}, bf16[2,128,8,128]{3,1,2,0:T(8,128)(2,1)}, u32[]{:S(2)}, u32[]{:S(2)}) collective-permute-start(bf16[2,128,8,128]{3,1,2,0:T(8,128)(2,1)} %pad_maximum_fusion.1), channel_id=1, source_target_pairs={{4,0},{8,4},{12,8},{16,12},{20,16},{24,20},{28,24},{32,28},{36,32}... | collective-permute-start | bytes 1572872 | tf_op jit(solution)/shard_map/ppermute | solution.py:16
  62.7 26.7 %collective-permute-start.7 = (bf16[2,128,8,128]{3,1,2,0:T(8,128)(2,1)}, bf16[2,128,8,128]{3,1,2,0:T(8,128)(2,1)}, u32[]{:S(2)}, u32[]{:S(2)}) collective-permute-start(bf16[2,128,8,128]{3,1,2,0:T(8,128)(2,1)} %pad_maximum_fusion.2), channel_id=1, source_target_pairs={{8,0},{12,4},{16,8},{20,12},{24,16},{28,20},{32,24},{36,28},{40,32... | collective-permute-start | bytes 1572872 | tf_op jit(solution)/shard_map/ppermute | solution.py:16
  66.4 0.7 copy-start.5
  66.4 0.7 copy-start.7
  72.8 5.0 %copy-start.4 = (f32[128,8,128]{2,0,1:T(8,128)S(1)}, f32[128,8,128]{2,0,1:T(8,128)}, u32[]{:S(2)}) copy-start(f32[128,8,128]{2,0,1:T(8,128)} %fusion.14) | copy-start | bytes 1572868
  73.2 16.2 %collective-permute-start.5 = (bf16[8,128,128]{2,1,0:T(8,128)(2,1)S(1)}, bf16[8,128,128]{2,1,0:T(8,128)(2,1)S(1)}, u32[]{:S(2)}, u32[]{:S(2)}) collective-permute-start(bf16[8,128,128]{2,1,0:T(8,128)(2,1)S(1)} %get-tuple-element.86), channel_id=1, source_target_pairs={{4,0},{8,4},{12,8},{16,12},{20,16},{24,20},{28,24},{32,28},{36,32}... | collective-permute-start | bytes 786440 | tf_op jit(solution)/shard_map/ppermute | solution.py:16
  89.4 2.0 %copy-start.6 = (bf16[8,128,128]{2,1,0:T(8,128)(2,1)S(1)}, bf16[8,128,128]{2,1,0:T(8,128)(2,1)}, u32[]{:S(2)}) copy-start(bf16[8,128,128]{2,1,0:T(8,128)(2,1)} %copy-done.5) | copy-start | bytes 786436
  89.5 11.6 %collective-permute-start.8 = (bf16[8,128,128]{2,1,0:T(8,128)(2,1)S(1)}, bf16[8,128,128]{2,1,0:T(8,128)(2,1)S(1)}, u32[]{:S(2)}, u32[]{:S(2)}) collective-permute-start(bf16[8,128,128]{2,1,0:T(8,128)(2,1)S(1)} %get-tuple-element.49), channel_id=1, source_target_pairs={{8,0},{12,4},{16,8},{20,12},{24,16},{28,20},{32,24},{36,28},{40,32... | collective-permute-start | bytes 786440 | tf_op jit(solution)/shard_map/ppermute | solution.py:16
  101.2 13.1 %collective-permute-start.9 = (bf16[8,128,128]{2,1,0:T(8,128)(2,1)S(1)}, bf16[8,128,128]{2,1,0:T(8,128)(2,1)S(1)}, u32[]{:S(2)}, u32[]{:S(2)}) collective-permute-start(bf16[8,128,128]{2,1,0:T(8,128)(2,1)S(1)} %fusion.55), channel_id=1, source_target_pairs={{16,0},{20,4},{24,8},{28,12},{32,16},{36,20},{40,24},{44,28},{48,3... | collective-permute-start | bytes 786440 | tf_op jit(solution)/shard_map/ppermute | solution.py:16
  114.4 12.9 %collective-permute-start.11 = (bf16[8,128,128]{2,1,0:T(8,128)(2,1)S(1)}, bf16[8,128,128]{2,1,0:T(8,128)(2,1)S(1)}, u32[]{:S(2)}, u32[]{:S(2)}) collective-permute-start(bf16[8,128,128]{2,1,0:T(8,128)(2,1)S(1)} %add_convert_fusion), channel_id=1, source_target_pairs={{36,0},{40,4},{44,8},{48,12},{52,16},{56,20},{60,24},{64,28},{68,3... | collective-permute-start | bytes 786440 | tf_op jit(solution)/shard_map/ppermute | solution.py:16
  116.3 13.7 %collective-permute-start.10 = (bf16[8,128,128]{2,1,0:T(8,128)(2,1)S(1)}, bf16[8,128,128]{2,1,0:T(8,128)(2,1)S(1)}, u32[]{:S(2)}, u32[]{:S(2)}) collective-permute-start(bf16[8,128,128]{2,1,0:T(8,128)(2,1)S(1)} %add_convert_fusion), channel_id=1, source_target_pairs={{4,0},{8,4},{12,8},{16,12},{20,16},{24,20},{28,24},{32,28},{36,32}... | collective-permute-start | bytes 786440 | tf_op jit(solution)/shard_map/ppermute | solution.py:16
